TPU v7x, 256 devices: a whole 4x4x8 slice. The times are simulated.
256 devices in a mesh: section: 8 (over x, core), dp: 32 (over y, z).
Axes of the slice: x: 4, y: 4, z: 8, core: 2. Of those that a mesh axis runs over, the one named last changes fastest.
Arguments:
- resid_in: bfloat16 [4, 1024, 2048], P(None, 'dp'), may hold values from -10 to 10
- dest_row: int32 [4, 1024], replicated, may hold values from 0 to 1023, as said below
- doc_ids: int32 [4, 1024], P(None, 'dp'), may hold values from 0 to 1023, as said below
- cotangent: bfloat16 [4, 1024, 2048], P(None, 'dp'), may hold values from -0.119628906 to 0.119628906
- gain: float32 [8, 2048], P('section'), may hold values from 0.5 to 1.5
- steer: float32 [8, 2048], P('section'), may hold values from -3 to 3
- w_query: bfloat16 [8, 2048, 1024], P('section', 'dp'), may hold values from -1 to 1
- w_keyval: bfloat16 [8, 2048, 512], P('section', 'dp'), may hold values from -1 to 1
- w_out: bfloat16 [8, 1024, 2048], P('section', None, 'dp'), may hold values from -0.1875 to 0.1875
Outputs:
- hidden_out: bfloat16 [8, 4, 1024, 2048], P('section', None, 'dp')
- grad_steer: float32 [8, 2048], P('section')
Inputs may be any that keep to these rules, and one draw needn't show every extreme that they name: Each row of dest_row is a permutation of 0 to 1023. Counting the tokens of one aligned block of 32 input tokens that go to one aligned block of 32 packed rows, no count exceeds 2, and some reach it in every micro-batch. doc_ids never falls along a row; every value is a row index r at which doc_ids equals r; each aligned block of 32 rows begins a document, so no document crosses such a block.
All inputs are finite; a program needn't handle non-finite values.
Results may differ from a plain program's by a relative error of at most 0.02.
Values may be sent and summed in bfloat16 or wider, within the bound.
No kernel may reach another device: no remote copies, remote signals or barrier semaphores. Data moves between devices by JAX's collectives and lax.ppermute only.
A program may use at most 64 MiB of HBM per device.

v0:
```python
import jax
import jax.numpy as jnp
from jax import lax
from jax.sharding import PartitionSpec as P

HD = 64
ROPE_BASE = 500000.0
EPSILON = 1e-05
MASKED = -1e30


def rope_tables(positions):
    half_size = HD // 2
    freq_index = jnp.arange(half_size, dtype=jnp.float32)
    inverse = ROPE_BASE ** (-2.0 * freq_index / HD)
    angles = positions.astype(jnp.float32)[..., None] * inverse
    return (jnp.cos(angles)[..., None, :], jnp.sin(angles)[..., None, :])


def rotate(values, tables):
    half_size = values.shape[-1] // 2
    cosine, sine_part = tables
    first_half = values[..., :half_size]
    second = values[..., half_size:]
    return jnp.concatenate(
        [first_half * cosine - second * sine_part, second * cosine + first_half * sine_part],
        axis=-1,
    )


def normalize(hidden_in, steering, gain_row):
    residual = hidden_in.astype(jnp.float32) + steering
    normed = (
        residual
        * lax.rsqrt(jnp.mean(residual * residual, axis=-1, keepdims=True) + EPSILON)
        * gain_row
    ).astype(jnp.bfloat16)
    return (residual, normed)


def attend(projected_in, tables, allowed, query_heads):
    row_count = projected_in.shape[0]
    head_size = HD
    query_cols = query_heads * head_size
    kv_heads = (projected_in.shape[1] - query_cols) // (2 * head_size)
    group_size = query_heads // kv_heads
    queries = projected_in[:, :query_cols].reshape(row_count, query_heads, head_size)
    keyval = projected_in[:, query_cols:]
    key_rows = rotate(
        keyval[:, : kv_heads * head_size].reshape(row_count, kv_heads, head_size), tables
    ).astype(jnp.bfloat16)
    values = (
        keyval[:, kv_heads * head_size :]
        .reshape(row_count, kv_heads, head_size)
        .astype(jnp.bfloat16)
    )
    queries = (
        rotate(queries, tables)
        .astype(jnp.bfloat16)
        .reshape(row_count, kv_heads, group_size, head_size)
    )
    scores = jnp.einsum(
        "rkgd,skd->kgrs", queries, key_rows, preferred_element_type=jnp.float32
    ) * head_size ** (-0.5)
    scores = jnp.where(allowed[None, None], scores, MASKED)
    peak = jnp.max(scores, axis=-1, keepdims=True)
    weights = jnp.exp(scores - peak)
    weights = (weights / jnp.sum(weights, axis=-1, keepdims=True)).astype(jnp.bfloat16)
    mixed_heads = jnp.einsum(
        "kgrs,skd->rkgd", weights, values, preferred_element_type=jnp.float32
    ).astype(jnp.bfloat16)
    return mixed_heads.reshape(row_count, query_heads * head_size)


def project_in(normed, w_qkv):
    return jnp.dot(normed, w_qkv, preferred_element_type=jnp.float32)


def project_out(residual, mixed_heads, w_out):
    return (residual + jnp.dot(mixed_heads, w_out, preferred_element_type=jnp.float32)).astype(
        jnp.bfloat16
    )


def layer_forward(hidden_in, steering, gain_row, w_qkv, w_out, tables, allowed):
    residual, normed = normalize(hidden_in, steering, gain_row)
    projected_in = project_in(normed, w_qkv)
    mixed_heads = attend(projected_in, tables, allowed, w_out.shape[0] // HD)
    return (project_out(residual, mixed_heads, w_out), projected_in)


def layer_backward(
    hidden_in, steering, projected_in, upstream, gain_row, w_qkv, w_out, tables, allowed
):
    query_heads = w_out.shape[0] // HD
    (residual, normed), normalize_pull = jax.vjp(
        lambda h, s: normalize(h, s, gain_row), hidden_in, steering
    )
    mixed_heads, attend_pull = jax.vjp(
        lambda p: attend(p, tables, allowed, query_heads), projected_in
    )
    unused_out, out_pull = jax.vjp(lambda r, m: project_out(r, m, w_out), residual, mixed_heads)
    grad_residual, grad_mixed = out_pull(upstream)
    (grad_projected,) = attend_pull(grad_mixed)
    unused_proj, in_pull = jax.vjp(lambda n: project_in(n, w_qkv), normed)
    (grad_normed,) = in_pull(grad_projected)
    return normalize_pull((grad_residual, grad_normed))


def butterfly_sum(values, axis):
    count = lax.axis_size(axis)
    index = lax.axis_index(axis)
    stride = 1
    while stride < count:
        fan = 4 if count % (stride * 4) == 0 else 2
        local = index // stride % fan
        received = [values]
        for offset in range(1, fan):
            route = [
                (
                    i,
                    i // (stride * fan) * stride * fan
                    + (i // stride % fan ^ offset) * stride
                    + i % stride,
                )
                for i in range(count)
            ]
            received.append(lax.ppermute(values, axis, route))
        stacked = jnp.stack(received)
        ordered = [
            lax.dynamic_index_in_dim(stacked, local ^ m, 0, keepdims=False) for m in range(fan)
        ]
        if fan == 4:
            values = ordered[0] + ordered[1] + (ordered[2] + ordered[3])
        else:
            values = ordered[0] + ordered[1]
        stride *= fan
    return values


def plan_slots(target, device, row_count, capacity, dp_count):
    target_grid = target.reshape(dp_count, row_count)
    target_dev = target_grid // row_count
    target_off = target_grid % row_count
    row_order = jnp.arange(row_count, dtype=jnp.int32)
    matching = target_dev[:, :, None] == target_dev[:, None, :]
    earlier = row_order[None, :] < row_order[:, None]
    rank_ids = jnp.sum((matching & earlier[None]).astype(jnp.int32), axis=2)
    slot_ids = target_dev * capacity + rank_ids
    own_slot = lax.dynamic_index_in_dim(slot_ids, device, 0, keepdims=False)
    column_ids = jnp.arange(dp_count, dtype=jnp.int32)[:, None] * capacity + rank_ids
    landing = (target_dev == device)[None] & (target_off[None] == row_order[:, None, None])
    source_col = jnp.sum(jnp.where(landing, column_ids[None], 0), axis=(1, 2))
    return (own_slot, source_col)


def pack_rows(source_rows, own_slot, slot_count):
    selector = (jnp.arange(slot_count, dtype=jnp.int32)[:, None] == own_slot[None, :]).astype(
        jnp.bfloat16
    )
    return jnp.dot(selector, source_rows, preferred_element_type=jnp.float32).astype(jnp.bfloat16)


def unpack_rows(arrived, source_col):
    selector = (
        source_col[:, None] == jnp.arange(arrived.shape[0], dtype=jnp.int32)[None, :]
    ).astype(jnp.bfloat16)
    return jnp.dot(selector, arrived, preferred_element_type=jnp.float32).astype(jnp.bfloat16)


def body(resid_in, dest_row, doc_ids, cotangent, gain, steer, w_query, w_keyval, w_out):
    dp_count = lax.axis_size("dp")
    section_count = lax.axis_size("section")
    device = lax.axis_index("dp")
    section_idx = lax.axis_index("section")
    micro_count, row_count, width = resid_in.shape
    capacity = row_count // dp_count + 1
    slot_count = dp_count * capacity
    full_qkv = lax.all_gather(
        jnp.concatenate([w_query[0], w_keyval[0]], axis=1), "dp", axis=0, tiled=True
    )
    full_out = lax.all_gather(w_out[0], "dp", axis=1, tiled=True)
    gain_row = gain[0]
    steering = steer[0]
    plans = [
        plan_slots(dest_row[micro_idx], device, row_count, capacity, dp_count)
        for micro_idx in range(micro_count)
    ]
    packed = jnp.stack(
        [
            pack_rows(resid_in[micro_idx], plans[micro_idx][0], slot_count).reshape(
                dp_count, capacity, width
            )
            for micro_idx in range(micro_count)
        ],
        axis=1,
    )
    arrived = lax.all_to_all(packed, "dp", split_axis=0, concat_axis=0, tiled=True)
    grouped = jnp.stack(
        [
            unpack_rows(arrived[:, micro_idx].reshape(slot_count, width), plans[micro_idx][1])
            for micro_idx in range(micro_count)
        ]
    )
    global_rows = device * row_count + jnp.arange(row_count, dtype=jnp.int32)
    flat_count = micro_count * row_count
    tables = rope_tables((global_rows[None, :] - doc_ids).reshape(flat_count))
    micro_of = jnp.arange(flat_count, dtype=jnp.int32) // row_count
    doc_keys = doc_ids.reshape(flat_count) + micro_of * (dp_count * row_count)
    flat_index = jnp.arange(flat_count, dtype=jnp.int32)
    allowed = (doc_keys[:, None] == doc_keys[None, :]) & (
        flat_index[:, None] >= flat_index[None, :]
    )
    grouped = grouped.reshape(flat_count, width)
    cotangent = cotangent.reshape(flat_count, width)

    def run_layer(hidden_in, steer_vec):
        return layer_forward(hidden_in, steer_vec, gain_row, full_qkv, full_out, tables, allowed)

    zero_block = jnp.zeros((flat_count, width), jnp.bfloat16)
    zero_proj = jnp.zeros((flat_count, full_qkv.shape[1]), jnp.float32)

    def precompute(hidden_in):
        return project_in(normalize(hidden_in, steering, gain_row)[1], full_qkv)

    forward_route = [(i, i + 1) for i in range(section_count - 1)]
    backward_route = [(i + 1, i) for i in range(section_count - 1)]

    def forward_step(carry, unused):
        hidden_in, kept, produced, step = carry
        active = section_idx == step
        kept = jnp.where(active, hidden_in, kept)
        hidden_new = lax.cond(active, lambda: run_layer(hidden_in, steering)[0], lambda: zero_block)
        produced = jnp.where(active, hidden_new, produced)
        sent = lax.ppermute(hidden_new, "section", forward_route)
        return ((sent, kept, produced, step + 1), None)

    (unused_in, kept, produced, unused_step), unused_ys = lax.scan(
        forward_step, (grouped, zero_block, zero_block, jnp.int32(0)), None, length=section_count
    )
    first_saved = lax.cond(
        section_idx == section_count - 1, lambda: precompute(kept), lambda: zero_proj
    )

    def backward_step(carry, unused):
        upstream, grad_sum, step, saved = carry
        active = section_idx == step

        def differentiate():
            return layer_backward(
                kept, steering, saved, upstream, gain_row, full_qkv, full_out, tables, allowed
            )

        grad_in, steer_part = lax.cond(
            active, differentiate, lambda: (zero_block, jnp.zeros_like(steering))
        )
        sent = lax.ppermute(grad_in, "section", backward_route)
        next_saved = lax.cond(section_idx == step - 1, lambda: precompute(kept), lambda: zero_proj)
        return ((sent, grad_sum + steer_part, step - 1, next_saved), None)

    (unused_grad, grad_sum, unused_step, unused_saved), unused_zs = lax.scan(
        backward_step,
        (cotangent, jnp.zeros_like(steering), jnp.int32(section_count - 1), first_saved),
        None,
        length=section_count,
    )
    total = butterfly_sum(grad_sum, "dp")
    return (produced.reshape(1, micro_count, row_count, width), total[None])


def solution(mesh):
    in_specs = (
        P(None, "dp", None),
        P(),
        P(None, "dp"),
        P(None, "dp", None),
        P("section", None),
        P("section", None),
        P("section", "dp", None),
        P("section", "dp", None),
        P("section", None, "dp"),
    )
    out_specs = (P("section", None, "dp", None), P("section", None))
    return jax.shard_map(body, mesh=mesh, in_specs=in_specs, out_specs=out_specs, check_vma=False)
```

profile of v0, /device:TPU:2, one launch (start us, length us, event | category | flops | bytes accessed | tf_op | source)
XLA Modules:
  0.0 510.0 jit_solution(17521883404294243884)
XLA Ops:
  21.6 11.7 %all-to-all-start = ((bf16[32,4,2,2048]{3,2,1,0:T(2,128)(2,1)}), bf16[32,4,2,2048]{3,2,1,0:T(2,128)(2,1)S(1)}, u32[]{:S(2)}, u32[]{:S(2)}) async-start(bf16[32,4,2,2048]{3,2,1,0:T(2,128)(2,1)} %pad_maximum_fusion.3), calls=%async_computation | async-start | bytes 2097152 | tf_op jit(solution)/shard_map/all_to_all | solution.py:198
  38.0 27.3 %all-to-all-done = bf16[32,4,2,2048]{3,2,1,0:T(2,128)(2,1)S(1)} async-done(((bf16[32,4,2,2048]{3,2,1,0:T(2,128)(2,1)}), bf16[32,4,2,2048]{3,2,1,0:T(2,128)(2,1)S(1)}, u32[]{:S(2)}, u32[]{:S(2)}) %all-to-all-start) | async-done | bytes 1048608 | tf_op jit(solution)/shard_map/all_to_all | solution.py:198
  67.5 31.5 %all-gather.6.cloned.1.call-done = bf16[1,1024,2048]{1,2,0:T(8,128)(2,1)} async-done(((bf16[1,1024,64]{1,2,0:T(8,128)(2,1)}), bf16[1,1024,2048]{1,2,0:T(8,128)(2,1)}) %all-gather.6.cloned.1.call-update) | async-done | bytes 4194320 | tf_op jit(solution)/shard_map/all_gather | solution.py:182
  99.0 6.5 %copy.55 = bf16[1024,2048]{1,0:T(8,128)(2,1)} copy(bf16[1024,2048]{0,1:T(8,128)(2,1)} %bitcast.223) | data formatting | bytes 8388608
  105.6 81.7 %all-gather.4.cloned.1.call-done = bf16[2048,1536]{1,0:T(8,128)(2,1)} async-done(((bf16[64,1536]{1,0:T(8,128)(2,1)}), bf16[2048,1536]{1,0:T(8,128)(2,1)}) %all-gather.4.cloned.1.call-update) | async-done | bytes 6291472 | tf_op jit(solution)/shard_map/all_gather | solution.py:179
  187.3 115.0 %while.42 = (s32[]{:T(128)}, bf16[128,2048]{1,0:T(8,128)(2,1)S(1)}, bf16[128,2048]{1,0:T(8,128)(2,1)S(1)}, bf16[128,2048]{1,0:T(8,128)(2,1)S(1)}, s32[]{:T(128)}...) while((s32[]{:T(128)}, bf16[128,2048]{1,0:T(8,128)(2,1)S(1)}, ...), condition=%wide.region_14.15_spmd.clone.clone.clone, body=%wide.region_8.14_spmd.clone.clone.clone.sunk | while | flops 1451809152 | bytes 27381680 | solution.py:238
  190.4 8.2 %collective-permute-done = bf16[128,2048]{1,0:T(8,128)(2,1)S(1)} collective-permute-done((bf16[128,2048]{1,0:T(8,128)(2,1)S(1)}, bf16[128,2048]{1,0:T(8,128)(2,1)S(1)}, u32[]{:S(2)}, u32[]{:S(2)}) %collective-permute-start) | collective-permute-done | bytes 524320 | tf_op jit(solution)/shard_map/while/body/eval_jaxpr/ppermute | solution.py:235
  201.9 18.8 %collective-permute-done = bf16[128,2048]{1,0:T(8,128)(2,1)S(1)} collective-permute-done((bf16[128,2048]{1,0:T(8,128)(2,1)S(1)}, bf16[128,2048]{1,0:T(8,128)(2,1)S(1)}, u32[]{:S(2)}, u32[]{:S(2)}) %collective-permute-start) | collective-permute-done | bytes 524320 | tf_op jit(solution)/shard_map/while/body/eval_jaxpr/ppermute | solution.py:235
  221.5 9.8 %conditional.17 = (bf16[128,2048]{1,0:T(8,128)(2,1)S(1)}) conditional(s32[]{:T(128)} %convert_element_type.348, () %tuple.183, (bf16[128,2048]{1,0:T(8,128)(2,1)S(1)}, f32[1,2048]{1,0:T(1,128)S(1)}, f32[1,2048]{1,0:T(1,128)S(1)}, bf16[2048,1536]{1,0:T(8,128)(2,1)}, s32[128]{0:T(128)}, /*index=5*/f32[128,1,32]{0,2,1:T(8,128)S(1)}, ...), branch_computations={%region_9.9_spmd, %region_10.13_spmd} | conditional | flops 1450756480 | bytes 20941832 | solution.py:233
  221.7 3.8 fusion.18
  233.6 8.2 %collective-permute-done = bf16[128,2048]{1,0:T(8,128)(2,1)S(1)} collective-permute-done((bf16[128,2048]{1,0:T(8,128)(2,1)S(1)}, bf16[128,2048]{1,0:T(8,128)(2,1)S(1)}, u32[]{:S(2)}, u32[]{:S(2)}) %collective-permute-start) | collective-permute-done | bytes 524320 | tf_op jit(solution)/shard_map/while/body/eval_jaxpr/ppermute | solution.py:235
  242.7 5.0 collective-permute-start
  248.1 5.2 %collective-permute-done = bf16[128,2048]{1,0:T(8,128)(2,1)S(1)} collective-permute-done((bf16[128,2048]{1,0:T(8,128)(2,1)S(1)}, bf16[128,2048]{1,0:T(8,128)(2,1)S(1)}, u32[]{:S(2)}, u32[]{:S(2)}) %collective-permute-start) | collective-permute-done | bytes 524320 | tf_op jit(solution)/shard_map/while/body/eval_jaxpr/ppermute | solution.py:235
  257.0 7.6 %collective-permute-done = bf16[128,2048]{1,0:T(8,128)(2,1)S(1)} collective-permute-done((bf16[128,2048]{1,0:T(8,128)(2,1)S(1)}, bf16[128,2048]{1,0:T(8,128)(2,1)S(1)}, u32[]{:S(2)}, u32[]{:S(2)}) %collective-permute-start) | collective-permute-done | bytes 524320 | tf_op jit(solution)/shard_map/while/body/eval_jaxpr/ppermute | solution.py:235
  265.6 12.2 %collective-permute-start = (bf16[128,2048]{1,0:T(8,128)(2,1)S(1)}, bf16[128,2048]{1,0:T(8,128)(2,1)S(1)}, u32[]{:S(2)}, u32[]{:S(2)}) collective-permute-start(bf16[128,2048]{1,0:T(8,128)(2,1)S(1)} %get-tuple-element.1353), channel_id=1, source_target_pairs={{0,32},{32,64},{64,96},{96,128},{128,160},{160,192},{192,224},{1,3... | collective-permute-start | bytes 1572872 | tf_op jit(solution)/shard_map/while/body/eval_jaxpr/ppermute | solution.py:235
  280.3 9.0 %collective-permute-start = (bf16[128,2048]{1,0:T(8,128)(2,1)S(1)}, bf16[128,2048]{1,0:T(8,128)(2,1)S(1)}, u32[]{:S(2)}, u32[]{:S(2)}) collective-permute-start(bf16[128,2048]{1,0:T(8,128)(2,1)S(1)} %get-tuple-element.1353), channel_id=1, source_target_pairs={{0,32},{32,64},{64,96},{96,128},{128,160},{160,192},{192,224},{1,3... | collective-permute-start | bytes 1572872 | tf_op jit(solution)/shard_map/while/body/eval_jaxpr/ppermute | solution.py:235
  291.7 9.0 %collective-permute-start = (bf16[128,2048]{1,0:T(8,128)(2,1)S(1)}, bf16[128,2048]{1,0:T(8,128)(2,1)S(1)}, u32[]{:S(2)}, u32[]{:S(2)}) collective-permute-start(bf16[128,2048]{1,0:T(8,128)(2,1)S(1)} %get-tuple-element.1353), channel_id=1, source_target_pairs={{0,32},{32,64},{64,96},{96,128},{128,160},{160,192},{192,224},{1,3... | collective-permute-start | bytes 1572872 | tf_op jit(solution)/shard_map/while/body/eval_jaxpr/ppermute | solution.py:235
  303.7 174.6 %while.43 = (s32[]{:T(128)}, bf16[128,2048]{1,0:T(8,128)(2,1)S(1)}, f32[2048]{0:T(1024)S(1)}, f32[128,1536]{1,0:T(8,128)}, s32[]{:T(128)}, /*index=5*/bf16[1024,...) while((s32[]{:T(128)}, bf16[128,2048]{1,0:T(8,128)(2,1)S(1)}, ...), condition=%wide.region_32.33_spmd.clone.clone.clone, body=%wide.region_18.32_spmd.clone.clone.clone.sunk | while | flops 2336233984 | bytes 65241192 | solution.py:261
  307.5 7.5 %collective-permute-done.1 = bf16[128,2048]{1,0:T(8,128)(2,1)S(1)} collective-permute-done((bf16[128,2048]{1,0:T(8,128)(2,1)S(1)}, bf16[128,2048]{1,0:T(8,128)(2,1)S(1)}, u32[]{:S(2)}, u32[]{:S(2)}) %collective-permute-start.1) | collective-permute-done | bytes 524320 | tf_op jit(solution)/shard_map/while/body/eval_jaxpr/ppermute | solution.py:257
  318.9 11.4 %collective-permute-done.1 = bf16[128,2048]{1,0:T(8,128)(2,1)S(1)} collective-permute-done((bf16[128,2048]{1,0:T(8,128)(2,1)S(1)}, bf16[128,2048]{1,0:T(8,128)(2,1)S(1)}, u32[]{:S(2)}, u32[]{:S(2)}) %collective-permute-start.1) | collective-permute-done | bytes 524320 | tf_op jit(solution)/shard_map/while/body/eval_jaxpr/ppermute | solution.py:257
  334.1 7.6 %collective-permute-done.1 = bf16[128,2048]{1,0:T(8,128)(2,1)S(1)} collective-permute-done((bf16[128,2048]{1,0:T(8,128)(2,1)S(1)}, bf16[128,2048]{1,0:T(8,128)(2,1)S(1)}, u32[]{:S(2)}, u32[]{:S(2)}) %collective-permute-start.1) | collective-permute-done | bytes 524320 | tf_op jit(solution)/shard_map/while/body/eval_jaxpr/ppermute | solution.py:257
  345.4 8.2 %collective-permute-done.1 = bf16[128,2048]{1,0:T(8,128)(2,1)S(1)} collective-permute-done((bf16[128,2048]{1,0:T(8,128)(2,1)S(1)}, bf16[128,2048]{1,0:T(8,128)(2,1)S(1)}, u32[]{:S(2)}, u32[]{:S(2)}) %collective-permute-start.1) | collective-permute-done | bytes 524320 | tf_op jit(solution)/shard_map/while/body/eval_jaxpr/ppermute | solution.py:257
  356.5 5.0 conditional.19
  356.7 4.7 fusion.69
  361.4 59.3 %collective-permute-done.1 = bf16[128,2048]{1,0:T(8,128)(2,1)S(1)} collective-permute-done((bf16[128,2048]{1,0:T(8,128)(2,1)S(1)}, bf16[128,2048]{1,0:T(8,128)(2,1)S(1)}, u32[]{:S(2)}, u32[]{:S(2)}) %collective-permute-start.1) | collective-permute-done | bytes 524320 | tf_op jit(solution)/shard_map/while/body/eval_jaxpr/ppermute | solution.py:257
  421.5 12.8 %conditional.18 = (bf16[128,2048]{1,0:T(8,128)(2,1)S(1)}, f32[2048]{0:T(1024)S(1)}) conditional(s32[]{:T(128)} %convert_element_type.349, () %tuple.186, (bf16[128,2048]{1,0:T(8,128)(2,1)S(1)}, bf16[1024,2048]{1,0:T(8,128)(2,1)}, s32[128]{0:T(128)}, f32[128,1536]{1,0:T(8,128)}, f32[128,1,32]{0,2,1:T(8,128)S(1)}, ...), branch_computations={%region_19.19_spmd, %region_20.28_spmd} | conditional | flops 1528560128 | bytes 54817856 | solution.py:254
  437.2 5.7 %collective-permute-done.1 = bf16[128,2048]{1,0:T(8,128)(2,1)S(1)} collective-permute-done((bf16[128,2048]{1,0:T(8,128)(2,1)S(1)}, bf16[128,2048]{1,0:T(8,128)(2,1)S(1)}, u32[]{:S(2)}, u32[]{:S(2)}) %collective-permute-start.1) | collective-permute-done | bytes 524320 | tf_op jit(solution)/shard_map/while/body/eval_jaxpr/ppermute | solution.py:257
  443.7 16.5 %collective-permute-start.1 = (bf16[128,2048]{1,0:T(8,128)(2,1)S(1)}, bf16[128,2048]{1,0:T(8,128)(2,1)S(1)}, u32[]{:S(2)}, u32[]{:S(2)}) collective-permute-start(bf16[128,2048]{1,0:T(8,128)(2,1)S(1)} %get-tuple-element.1250), channel_id=1, source_target_pairs={{32,0},{64,32},{96,64},{128,96},{160,128},{192,160},{224,192},{33,... | collective-permute-start | bytes 1572872 | tf_op jit(solution)/shard_map/while/body/eval_jaxpr/ppermute | solution.py:257
  461.2 5.7 %collective-permute-done.1 = bf16[128,2048]{1,0:T(8,128)(2,1)S(1)} collective-permute-done((bf16[128,2048]{1,0:T(8,128)(2,1)S(1)}, bf16[128,2048]{1,0:T(8,128)(2,1)S(1)}, u32[]{:S(2)}, u32[]{:S(2)}) %collective-permute-start.1) | collective-permute-done | bytes 524320 | tf_op jit(solution)/shard_map/while/body/eval_jaxpr/ppermute | solution.py:257
  467.8 3.8 collective-permute-start.1
  472.6 5.7 %collective-permute-done.1 = bf16[128,2048]{1,0:T(8,128)(2,1)S(1)} collective-permute-done((bf16[128,2048]{1,0:T(8,128)(2,1)S(1)}, bf16[128,2048]{1,0:T(8,128)(2,1)S(1)}, u32[]{:S(2)}, u32[]{:S(2)}) %collective-permute-start.1) | collective-permute-done | bytes 524320 | tf_op jit(solution)/shard_map/while/body/eval_jaxpr/ppermute | solution.py:257
  498.8 3.7 collective-permute-done.8
  (274 shorter events, 117.6 us)
Async XLA Ops:
  7.2 26.1 %copy-start.5 = (s32[4,32]{1,0:T(4,128)S(1)}, s32[4,32]{1,0:T(4,128)}, u32[]{:S(2)}) copy-start(s32[4,32]{1,0:T(4,128)} %param.23) | copy-start | bytes 1540
  7.2 91.9 %all-gather.6.cloned.1.call-start = ((), (), s32[]{:S(2)}) async-start(), calls=%async_computation.2 | async-start | bytes 4325376 | tf_op jit(solution)/shard_map/all_gather | solution.py:182
  7.9 179.4 %all-gather.4.cloned.1.call-start = ((), (), s32[]{:S(2)}) async-start(), calls=%async_computation.1 | async-start | bytes 6488064 | tf_op jit(solution)/shard_map/all_gather | solution.py:179
  21.6 43.7 %all-to-all-start = ((bf16[32,4,2,2048]{3,2,1,0:T(2,128)(2,1)}), bf16[32,4,2,2048]{3,2,1,0:T(2,128)(2,1)S(1)}, u32[]{:S(2)}, u32[]{:S(2)}) async-start(bf16[32,4,2,2048]{3,2,1,0:T(2,128)(2,1)} %pad_maximum_fusion.3), calls=%async_computation | async-start | bytes 2097152 | tf_op jit(solution)/shard_map/all_to_all | solution.py:198
  66.2 121.1 %copy-start.2 = (f32[1,2048]{1,0:T(1,128)S(1)}, f32[1,2048]{1,0:T(1,128)}, u32[]{:S(2)}) copy-start(f32[1,2048]{1,0:T(1,128)} %param.26) | copy-start | bytes 24580
  66.2 121.1 %copy-start.3 = (f32[1,2048]{1,0:T(1,128)S(1)}, f32[1,2048]{1,0:T(1,128)}, u32[]{:S(2)}) copy-start(f32[1,2048]{1,0:T(1,128)} %param.25) | copy-start | bytes 24580
  188.1 10.5 %collective-permute-start = (bf16[128,2048]{1,0:T(8,128)(2,1)S(1)}, bf16[128,2048]{1,0:T(8,128)(2,1)S(1)}, u32[]{:S(2)}, u32[]{:S(2)}) collective-permute-start(bf16[128,2048]{1,0:T(8,128)(2,1)S(1)} %get-tuple-element.1353), channel_id=1, source_target_pairs={{0,32},{32,64},{64,96},{96,128},{128,160},{160,192},{192,224},{1,3... | collective-permute-start | bytes 1572872 | tf_op jit(solution)/shard_map/while/body/eval_jaxpr/ppermute | solution.py:235
  199.6 21.1 %collective-permute-start = (bf16[128,2048]{1,0:T(8,128)(2,1)S(1)}, bf16[128,2048]{1,0:T(8,128)(2,1)S(1)}, u32[]{:S(2)}, u32[]{:S(2)}) collective-permute-start(bf16[128,2048]{1,0:T(8,128)(2,1)S(1)} %get-tuple-element.1353), channel_id=1, source_target_pairs={{0,32},{32,64},{64,96},{96,128},{128,160},{160,192},{192,224},{1,3... | collective-permute-start | bytes 1572872 | tf_op jit(solution)/shard_map/while/body/eval_jaxpr/ppermute | solution.py:235
  231.3 10.5 %collective-permute-start = (bf16[128,2048]{1,0:T(8,128)(2,1)S(1)}, bf16[128,2048]{1,0:T(8,128)(2,1)S(1)}, u32[]{:S(2)}, u32[]{:S(2)}) collective-permute-start(bf16[128,2048]{1,0:T(8,128)(2,1)S(1)} %get-tuple-element.1353), channel_id=1, source_target_pairs={{0,32},{32,64},{64,96},{96,128},{128,160},{160,192},{192,224},{1,3... | collective-permute-start | bytes 1572872 | tf_op jit(solution)/shard_map/while/body/eval_jaxpr/ppermute | solution.py:235
  242.7 10.5 %collective-permute-start = (bf16[128,2048]{1,0:T(8,128)(2,1)S(1)}, bf16[128,2048]{1,0:T(8,128)(2,1)S(1)}, u32[]{:S(2)}, u32[]{:S(2)}) collective-permute-start(bf16[128,2048]{1,0:T(8,128)(2,1)S(1)} %get-tuple-element.1353), channel_id=1, source_target_pairs={{0,32},{32,64},{64,96},{96,128},{128,160},{160,192},{192,224},{1,3... | collective-permute-start | bytes 1572872 | tf_op jit(solution)/shard_map/while/body/eval_jaxpr/ppermute | solution.py:235
  254.2 10.5 %collective-permute-start = (bf16[128,2048]{1,0:T(8,128)(2,1)S(1)}, bf16[128,2048]{1,0:T(8,128)(2,1)S(1)}, u32[]{:S(2)}, u32[]{:S(2)}) collective-permute-start(bf16[128,2048]{1,0:T(8,128)(2,1)S(1)} %get-tuple-element.1353), channel_id=1, source_target_pairs={{0,32},{32,64},{64,96},{96,128},{128,160},{160,192},{192,224},{1,3... | collective-permute-start | bytes 1572872 | tf_op jit(solution)/shard_map/while/body/eval_jaxpr/ppermute | solution.py:235
  265.6 13.7 %collective-permute-start = (bf16[128,2048]{1,0:T(8,128)(2,1)S(1)}, bf16[128,2048]{1,0:T(8,128)(2,1)S(1)}, u32[]{:S(2)}, u32[]{:S(2)}) collective-permute-start(bf16[128,2048]{1,0:T(8,128)(2,1)S(1)} %get-tuple-element.1353), channel_id=1, source_target_pairs={{0,32},{32,64},{64,96},{96,128},{128,160},{160,192},{192,224},{1,3... | collective-permute-start | bytes 1572872 | tf_op jit(solution)/shard_map/while/body/eval_jaxpr/ppermute | solution.py:235
  280.3 10.5 %collective-permute-start = (bf16[128,2048]{1,0:T(8,128)(2,1)S(1)}, bf16[128,2048]{1,0:T(8,128)(2,1)S(1)}, u32[]{:S(2)}, u32[]{:S(2)}) collective-permute-start(bf16[128,2048]{1,0:T(8,128)(2,1)S(1)} %get-tuple-element.1353), channel_id=1, source_target_pairs={{0,32},{32,64},{64,96},{96,128},{128,160},{160,192},{192,224},{1,3... | collective-permute-start | bytes 1572872 | tf_op jit(solution)/shard_map/while/body/eval_jaxpr/ppermute | solution.py:235
  291.7 10.5 %collective-permute-start = (bf16[128,2048]{1,0:T(8,128)(2,1)S(1)}, bf16[128,2048]{1,0:T(8,128)(2,1)S(1)}, u32[]{:S(2)}, u32[]{:S(2)}) collective-permute-start(bf16[128,2048]{1,0:T(8,128)(2,1)S(1)} %get-tuple-element.1353), channel_id=1, source_target_pairs={{0,32},{32,64},{64,96},{96,128},{128,160},{160,192},{192,224},{1,3... | collective-permute-start | bytes 1572872 | tf_op jit(solution)/shard_map/while/body/eval_jaxpr/ppermute | solution.py:235
  302.2 1.4 copy-start.1
  304.6 10.4 %collective-permute-start.1 = (bf16[128,2048]{1,0:T(8,128)(2,1)S(1)}, bf16[128,2048]{1,0:T(8,128)(2,1)S(1)}, u32[]{:S(2)}, u32[]{:S(2)}) collective-permute-start(bf16[128,2048]{1,0:T(8,128)(2,1)S(1)} %get-tuple-element.1250), channel_id=1, source_target_pairs={{32,0},{64,32},{96,64},{128,96},{160,128},{192,160},{224,192},{33,... | collective-permute-start | bytes 1572872 | tf_op jit(solution)/shard_map/while/body/eval_jaxpr/ppermute | solution.py:257
  315.8 14.5 %collective-permute-start.1 = (bf16[128,2048]{1,0:T(8,128)(2,1)S(1)}, bf16[128,2048]{1,0:T(8,128)(2,1)S(1)}, u32[]{:S(2)}, u32[]{:S(2)}) collective-permute-start(bf16[128,2048]{1,0:T(8,128)(2,1)S(1)} %get-tuple-element.1250), channel_id=1, source_target_pairs={{32,0},{64,32},{96,64},{128,96},{160,128},{192,160},{224,192},{33,... | collective-permute-start | bytes 1572872 | tf_op jit(solution)/shard_map/while/body/eval_jaxpr/ppermute | solution.py:257
  331.2 10.5 %collective-permute-start.1 = (bf16[128,2048]{1,0:T(8,128)(2,1)S(1)}, bf16[128,2048]{1,0:T(8,128)(2,1)S(1)}, u32[]{:S(2)}, u32[]{:S(2)}) collective-permute-start(bf16[128,2048]{1,0:T(8,128)(2,1)S(1)} %get-tuple-element.1250), channel_id=1, source_target_pairs={{32,0},{64,32},{96,64},{128,96},{160,128},{192,160},{224,192},{33,... | collective-permute-start | bytes 1572872 | tf_op jit(solution)/shard_map/while/body/eval_jaxpr/ppermute | solution.py:257
  342.5 11.1 %collective-permute-start.1 = (bf16[128,2048]{1,0:T(8,128)(2,1)S(1)}, bf16[128,2048]{1,0:T(8,128)(2,1)S(1)}, u32[]{:S(2)}, u32[]{:S(2)}) collective-permute-start(bf16[128,2048]{1,0:T(8,128)(2,1)S(1)} %get-tuple-element.1250), channel_id=1, source_target_pairs={{32,0},{64,32},{96,64},{128,96},{160,128},{192,160},{224,192},{33,... | collective-permute-start | bytes 1572872 | tf_op jit(solution)/shard_map/while/body/eval_jaxpr/ppermute | solution.py:257
  354.5 66.2 %collective-permute-start.1 = (bf16[128,2048]{1,0:T(8,128)(2,1)S(1)}, bf16[128,2048]{1,0:T(8,128)(2,1)S(1)}, u32[]{:S(2)}, u32[]{:S(2)}) collective-permute-start(bf16[128,2048]{1,0:T(8,128)(2,1)S(1)} %get-tuple-element.1250), channel_id=1, source_target_pairs={{32,0},{64,32},{96,64},{128,96},{160,128},{192,160},{224,192},{33,... | collective-permute-start | bytes 1572872 | tf_op jit(solution)/shard_map/while/body/eval_jaxpr/ppermute | solution.py:257
  428.5 2.7 slice-start
  429.3 2.2 slice-start.1
  434.3 8.6 %collective-permute-start.1 = (bf16[128,2048]{1,0:T(8,128)(2,1)S(1)}, bf16[128,2048]{1,0:T(8,128)(2,1)S(1)}, u32[]{:S(2)}, u32[]{:S(2)}) collective-permute-start(bf16[128,2048]{1,0:T(8,128)(2,1)S(1)} %get-tuple-element.1250), channel_id=1, source_target_pairs={{32,0},{64,32},{96,64},{128,96},{160,128},{192,160},{224,192},{33,... | collective-permute-start | bytes 1572872 | tf_op jit(solution)/shard_map/while/body/eval_jaxpr/ppermute | solution.py:257
  443.7 23.2 %collective-permute-start.1 = (bf16[128,2048]{1,0:T(8,128)(2,1)S(1)}, bf16[128,2048]{1,0:T(8,128)(2,1)S(1)}, u32[]{:S(2)}, u32[]{:S(2)}) collective-permute-start(bf16[128,2048]{1,0:T(8,128)(2,1)S(1)} %get-tuple-element.1250), channel_id=1, source_target_pairs={{32,0},{64,32},{96,64},{128,96},{160,128},{192,160},{224,192},{33,... | collective-permute-start | bytes 1572872 | tf_op jit(solution)/shard_map/while/body/eval_jaxpr/ppermute | solution.py:257
  467.8 10.5 %collective-permute-start.1 = (bf16[128,2048]{1,0:T(8,128)(2,1)S(1)}, bf16[128,2048]{1,0:T(8,128)(2,1)S(1)}, u32[]{:S(2)}, u32[]{:S(2)}) collective-permute-start(bf16[128,2048]{1,0:T(8,128)(2,1)S(1)} %get-tuple-element.1250), channel_id=1, source_target_pairs={{32,0},{64,32},{96,64},{128,96},{160,128},{192,160},{224,192},{33,... | collective-permute-start | bytes 1572872 | tf_op jit(solution)/shard_map/while/body/eval_jaxpr/ppermute | solution.py:257
  478.3 5.4 %collective-permute-start.4 = (f32[2048]{0:T(1024)S(1)}, f32[2048]{0:T(1024)S(1)}, u32[]{:S(2)}, u32[]{:S(2)}) collective-permute-start(f32[2048]{0:T(1024)S(1)} %get-tuple-element.619), channel_id=1, source_target_pairs={{0,3},{1,2},{2,1},{3,0},{4,7},{5,6},{6,5},{7,4},{8,11},{9,10},{10,... | collective-permute-start | bytes 24584 | tf_op jit(solution)/shard_map/ppermute | solution.py:128
  481.0 4.5 collective-permute-start.3
  481.2 4.3 collective-permute-start.2
  485.6 8.5 %collective-permute-start.7 = (f32[2048]{0:T(1024)S(1)}, f32[2048]{0:T(1024)S(1)}, u32[]{:S(2)}, u32[]{:S(2)}) collective-permute-start(f32[2048]{0:T(1024)S(1)} %bitcast.245), channel_id=1, source_target_pairs={{0,12},{1,13},{2,14},{3,15},{4,8},{5,9},{6,10},{7,11},{8,4},{9,5},... | collective-permute-start | bytes 24584 | tf_op jit(solution)/shard_map/ppermute | solution.py:128
  487.8 6.4 %collective-permute-start.6 = (f32[2048]{0:T(1024)S(1)}, f32[2048]{0:T(1024)S(1)}, u32[]{:S(2)}, u32[]{:S(2)}) collective-permute-start(f32[2048]{0:T(1024)S(1)} %bitcast.246), channel_id=1, source_target_pairs={{0,8},{1,9},{2,10},{3,11},{4,12},{5,13},{6,14},{7,15},{8,0},{9,1},... | collective-permute-start | bytes 24584 | tf_op jit(solution)/shard_map/ppermute | solution.py:128
  489.6 7.6 %collective-permute-start.5 = (f32[2048]{0:T(1024)S(1)}, f32[2048]{0:T(1024)S(1)}, u32[]{:S(2)}, u32[]{:S(2)}) collective-permute-start(f32[2048]{0:T(1024)S(1)} %bitcast.247), channel_id=1, source_target_pairs={{0,4},{1,5},{2,6},{3,7},{4,0},{5,1},{6,2},{7,3},{8,12},{9,13},{10,... | collective-permute-start | bytes 24584 | tf_op jit(solution)/shard_map/ppermute | solution.py:128
  497.2 5.2 %collective-permute-start.8 = (f32[2048]{0:T(1024)S(1)}, f32[2048]{0:T(1024)S(1)}, u32[]{:S(2)}, u32[]{:S(2)}) collective-permute-start(f32[2048]{0:T(1024)S(1)} %bitcast.244), channel_id=1, source_target_pairs={{0,16},{1,17},{2,18},{3,19},{4,20},{5,21},{6,22},{7,23},{8,24},{9,... | collective-permute-start | bytes 24584 | tf_op jit(solution)/shard_map/ppermute | solution.py:128
  (2 other events, 2.8 us)
Sparse Core Ops, SparseCore 0:
  10.6 88.4 all-gather.5
  102.2 85.0 all-gather.3
where the time goes:
time: 511 us; the launch traced here: 510 us
  waiting for transfers between devices  314 us (61%)
  starting transfers between devices  100 us (20%)
  other arithmetic  31.1 us (6%)
  matrix products  25.8 us (5%)
  local copies, waits for them, and re-layouts  22.5 us (4%)
  between operations  14.4 us (3%)
    ppermute x8, waiting for transfers between devices, backward_step(): sent = lax.ppermute(grad_in, 'section', backward_route)  111 us
    all_gather x1, waiting for transfers between devices, body(): lax.all_gather(jnp.concatenate([w_query[0], w_keyval[0]], axis=1), 'dp',...  81.7 us
    ppermute x8, waiting for transfers between devices, forward_step(): sent = lax.ppermute(hidden_new, 'section', forward_route)  51.4 us
    ppermute x8, starting transfers between devices, forward_step(): sent = lax.ppermute(hidden_new, 'section', forward_route)  43.4 us
    ppermute x8, starting transfers between devices, backward_step(): sent = lax.ppermute(grad_in, 'section', backward_route)  32 us
    all_gather x1, waiting for transfers between devices, body(): full_out = lax.all_gather(w_out[0], 'dp', axis=1, tiled=True)  31.5 us
    all_to_all x1, waiting for transfers between devices, body(): lax.all_to_all(packed, 'dp', split_axis=0, concat_axis=0, tiled=True)  27.3 us
    ppermute x7, starting transfers between devices, butterfly_sum(): received.append(lax.ppermute(values, axis, route))  13.4 us
  transfers between devices with their start and end apart: 26, of which 24 were waited for; matrix products, arithmetic and copies ran while one was open for 8% of the time, Pallas kernels for 0%

commit v1 on v0

--- a/solution.py
+++ b/solution.py
@@ -179,7 +179,9 @@
     full_qkv = lax.all_gather(
         jnp.concatenate([w_query[0], w_keyval[0]], axis=1), "dp", axis=0, tiled=True
     )
-    full_out = lax.all_gather(w_out[0], "dp", axis=1, tiled=True)
+    full_out = jnp.concatenate(
+        lax.all_to_all(jnp.stack([w_out[0]] * lax.axis_size("dp")), "dp", 0, 0), axis=1
+    )
     gain_row = gain[0]
     steering = steer[0]
     plans = [

time: 511 us -> 553 us (1.082)
  blocking collectives: 0 us -> 45.9 us
  waiting for transfers between devices: 314 us -> 282 us
  other arithmetic: 31.1 us -> 48.6 us
  local copies, waits for them, and re-layouts: 22.5 us -> 30.8 us
    all_to_all x1, waiting for transfers between devices: 27.3 us -> 115 us  [body(): lax.all_to_all(jnp.stack([w_out[0]] * lax.axis_size('dp')), 'dp', 0, 0)]
    all_gather x1, waiting for transfers between devices: 81.7 us -> 0.01 us  [body(): lax.all_gather(jnp.concatenate([w_query[0], w_keyval[0]], axis=1), 'dp',...]
    all_to_all x0 -> x1, blocking collectives: none -> 45.9 us  [body(): lax.all_to_all(packed, 'dp', split_axis=0, concat_axis=0, tiled=True)]
    all_gather x1 -> x0, waiting for transfers between devices: 31.5 us -> none  [body(): full_out = lax.all_gather(w_out[0], 'dp', axis=1, tiled=True)]
    select_n x8, other arithmetic: 2.87 us -> 16.3 us  [forward_step(): produced = jnp.where(active, hidden_new, produced)]
    ppermute x8, waiting for transfers between devices: 51.4 us -> 39.9 us  [forward_step(): sent = lax.ppermute(hidden_new, 'section', forward_route)]
    ppermute x8, waiting for transfers between devices: 111 us -> 118 us  [backward_step(): sent = lax.ppermute(grad_in, 'section', backward_route)]
    all_to_all x1, starting transfers between devices: 11.7 us -> 5.04 us  [body(): lax.all_to_all(jnp.stack([w_out[0]] * lax.axis_size('dp')), 'dp', 0, 0)]
  transfers between devices with their start and end apart: 26 -> 25, of which waited for: 24 -> 19; matrix products, arithmetic and copies ran while one was open for 8% -> 10% of each run, Pallas kernels for 0% -> 0%
where the time goes in v1:
time: 553 us; the launch traced here: 548 us
  waiting for transfers between devices  282 us (51%)
  starting transfers between devices  97.4 us (18%)
  other arithmetic  48.6 us (9%)
  blocking collectives  45.9 us (8%)
  local copies, waits for them, and re-layouts  30.8 us (6%)
  matrix products  27.8 us (5%)
  between operations  14.4 us (3%)
    ppermute x8, waiting for transfers between devices, backward_step(): sent = lax.ppermute(grad_in, 'section', backward_route)  118 us
    all_to_all x1, waiting for transfers between devices, body(): lax.all_to_all(jnp.stack([w_out[0]] * lax.axis_size('dp')), 'dp', 0, 0)  115 us
    all_to_all x1, blocking collectives, body(): lax.all_to_all(packed, 'dp', split_axis=0, concat_axis=0, tiled=True)  45.9 us
    ppermute x8, waiting for transfers between devices, forward_step(): sent = lax.ppermute(hidden_new, 'section', forward_route)  39.9 us
    ppermute x8, starting transfers between devices, forward_step(): sent = lax.ppermute(hidden_new, 'section', forward_route)  39.5 us
    ppermute x8, starting transfers between devices, backward_step(): sent = lax.ppermute(grad_in, 'section', backward_route)  35.1 us
    ppermute x7, starting transfers between devices, butterfly_sum(): received.append(lax.ppermute(values, axis, route))  17.7 us
    mul x16, other arithmetic, rope_tables(): angles = positions.astype(jnp.float32)[..., None] * inverse  16.8 us
  transfers between devices with their start and end apart: 25, of which 19 were waited for; matrix products, arithmetic and copies ran while one was open for 10% of the time, Pallas kernels for 0%

profile of v1, /device:TPU:2, one launch (start us, length us, event | category | flops | bytes accessed | tf_op | source)
XLA Modules:
  0.0 548.4 jit_solution(8661053694967328984)
XLA Ops:
  20.1 45.9 %all_to_all.10 = bf16[32,4,2,2048]{3,2,1,0:T(2,128)(2,1)S(1)} all-to-all(bf16[32,4,2,2048]{3,2,1,0:T(2,128)(2,1)S(1)} %pad_maximum_fusion.3), channel_id=1, replica_groups=mesh['section'=8,'dp'=32] {'dp'}, dimensions={0} | all-to-all | bytes 2097152 | tf_op jit(solution)/shard_map/all_to_all | solution.py:200
  68.6 5.0 all-to-all-start.1
  80.8 115.5 %all-to-all-done.1 = bf16[32,1024,64]{1,2,0:T(8,128)(2,1)} async-done(((bf16[32,1024,64]{1,2,0:T(8,128)(2,1)}), bf16[32,1024,64]{1,2,0:T(8,128)(2,1)}, u32[]{:S(2)}, u32[]{:S(2)}) %all-to-all-start.1) | async-done | bytes 4194336 | tf_op jit(solution)/shard_map/all_to_all | solution.py:183
  196.2 6.5 %copy.56 = bf16[1024,2048]{1,0:T(8,128)(2,1)} copy(bf16[1024,2048]{0,1:T(8,128)(2,1)} %bitcast.77) | data formatting | bytes 8388608
  202.8 117.0 %while.42 = (s32[]{:T(128)}, bf16[128,2048]{1,0:T(8,128)(2,1)S(1)}, bf16[128,2048]{1,0:T(8,128)(2,1)S(1)}, bf16[128,2048]{1,0:T(8,128)(2,1)}, s32[]{:T(128)}, /*...) while((s32[]{:T(128)}, bf16[128,2048]{1,0:T(8,128)(2,1)S(1)}, ...), condition=%wide.region_14.15_spmd.clone.clone.clone, body=%wide.region_8.14_spmd.clone.clone.clone.sunk | while | flops 1451809152 | bytes 27449312 | solution.py:240
  207.3 7.4 %collective-permute-done = bf16[128,2048]{1,0:T(8,128)(2,1)S(1)} collective-permute-done((bf16[128,2048]{1,0:T(8,128)(2,1)S(1)}, bf16[128,2048]{1,0:T(8,128)(2,1)S(1)}, u32[]{:S(2)}, u32[]{:S(2)}) %collective-permute-start) | collective-permute-done | bytes 524320 | tf_op jit(solution)/shard_map/while/body/eval_jaxpr/ppermute | solution.py:237
  220.4 15.7 %collective-permute-done = bf16[128,2048]{1,0:T(8,128)(2,1)S(1)} collective-permute-done((bf16[128,2048]{1,0:T(8,128)(2,1)S(1)}, bf16[128,2048]{1,0:T(8,128)(2,1)S(1)}, u32[]{:S(2)}, u32[]{:S(2)}) %collective-permute-start) | collective-permute-done | bytes 524320 | tf_op jit(solution)/shard_map/while/body/eval_jaxpr/ppermute | solution.py:237
  237.5 9.1 %conditional.17 = (bf16[128,2048]{1,0:T(8,128)(2,1)S(1)}) conditional(s32[]{:T(128)} %convert_element_type.348, () %tuple.185, (bf16[128,2048]{1,0:T(8,128)(2,1)S(1)}, f32[1,2048]{1,0:T(1,128)S(1)}, f32[1,2048]{1,0:T(1,128)S(1)}, bf16[2048,1536]{1,0:T(8,128)(2,1)}, s32[128]{0:T(128)}, /*index=5*/f32[128,1,32]{0,2,1:T(8,128)}, ...), branch_computations={%region_9.9_spmd, %region_10.13_spmd} | conditional | flops 1450756480 | bytes 21009472 | solution.py:235
  237.7 3.8 fusion.18
  250.7 6.4 %collective-permute-done = bf16[128,2048]{1,0:T(8,128)(2,1)S(1)} collective-permute-done((bf16[128,2048]{1,0:T(8,128)(2,1)S(1)}, bf16[128,2048]{1,0:T(8,128)(2,1)S(1)}, u32[]{:S(2)}, u32[]{:S(2)}) %collective-permute-start) | collective-permute-done | bytes 524320 | tf_op jit(solution)/shard_map/while/body/eval_jaxpr/ppermute | solution.py:237
  258.6 4.3 collective-permute-start
  265.1 4.0 collective-permute-done
  274.7 6.4 %collective-permute-done = bf16[128,2048]{1,0:T(8,128)(2,1)S(1)} collective-permute-done((bf16[128,2048]{1,0:T(8,128)(2,1)S(1)}, bf16[128,2048]{1,0:T(8,128)(2,1)S(1)}, u32[]{:S(2)}, u32[]{:S(2)}) %collective-permute-start) | collective-permute-done | bytes 524320 | tf_op jit(solution)/shard_map/while/body/eval_jaxpr/ppermute | solution.py:237
  282.7 10.9 %collective-permute-start = (bf16[128,2048]{1,0:T(8,128)(2,1)S(1)}, bf16[128,2048]{1,0:T(8,128)(2,1)S(1)}, u32[]{:S(2)}, u32[]{:S(2)}) collective-permute-start(bf16[128,2048]{1,0:T(8,128)(2,1)S(1)} %get-tuple-element.1378), channel_id=1, source_target_pairs={{0,32},{32,64},{64,96},{96,128},{128,160},{160,192},{192,224},{1,3... | collective-permute-start | bytes 1572872 | tf_op jit(solution)/shard_map/while/body/eval_jaxpr/ppermute | solution.py:237
  297.3 8.3 %collective-permute-start = (bf16[128,2048]{1,0:T(8,128)(2,1)S(1)}, bf16[128,2048]{1,0:T(8,128)(2,1)S(1)}, u32[]{:S(2)}, u32[]{:S(2)}) collective-permute-start(bf16[128,2048]{1,0:T(8,128)(2,1)S(1)} %get-tuple-element.1378), channel_id=1, source_target_pairs={{0,32},{32,64},{64,96},{96,128},{128,160},{160,192},{192,224},{1,3... | collective-permute-start | bytes 1572872 | tf_op jit(solution)/shard_map/while/body/eval_jaxpr/ppermute | solution.py:237
  309.3 8.3 %collective-permute-start = (bf16[128,2048]{1,0:T(8,128)(2,1)S(1)}, bf16[128,2048]{1,0:T(8,128)(2,1)S(1)}, u32[]{:S(2)}, u32[]{:S(2)}) collective-permute-start(bf16[128,2048]{1,0:T(8,128)(2,1)S(1)} %get-tuple-element.1378), channel_id=1, source_target_pairs={{0,32},{32,64},{64,96},{96,128},{128,160},{160,192},{192,224},{1,3... | collective-permute-start | bytes 1572872 | tf_op jit(solution)/shard_map/while/body/eval_jaxpr/ppermute | solution.py:237
  320.9 193.1 %while.43 = (s32[]{:T(128)}, bf16[128,2048]{1,0:T(8,128)(2,1)S(1)}, f32[2048]{0:T(1024)}, f32[128,1536]{1,0:T(8,128)}, s32[]{:T(128)}, /*index=5*/bf16[1024,2048...) while((s32[]{:T(128)}, bf16[128,2048]{1,0:T(8,128)(2,1)S(1)}, ...), condition=%wide.region_32.33_spmd.clone.clone.clone, body=%wide.region_18.32_spmd.clone.clone.clone.sunk | while | flops 2336233984 | bytes 66357492 | solution.py:263
  325.6 7.0 %collective-permute-done.1 = bf16[128,2048]{1,0:T(8,128)(2,1)S(1)} collective-permute-done((bf16[128,2048]{1,0:T(8,128)(2,1)}, bf16[128,2048]{1,0:T(8,128)(2,1)S(1)}, u32[]{:S(2)}, u32[]{:S(2)}) %collective-permute-start.1) | collective-permute-done | bytes 524320 | tf_op jit(solution)/shard_map/while/body/eval_jaxpr/ppermute | solution.py:259
  338.1 10.3 %collective-permute-done.1 = bf16[128,2048]{1,0:T(8,128)(2,1)S(1)} collective-permute-done((bf16[128,2048]{1,0:T(8,128)(2,1)}, bf16[128,2048]{1,0:T(8,128)(2,1)S(1)}, u32[]{:S(2)}, u32[]{:S(2)}) %collective-permute-start.1) | collective-permute-done | bytes 524320 | tf_op jit(solution)/shard_map/while/body/eval_jaxpr/ppermute | solution.py:259
  353.2 7.8 %collective-permute-done.1 = bf16[128,2048]{1,0:T(8,128)(2,1)S(1)} collective-permute-done((bf16[128,2048]{1,0:T(8,128)(2,1)}, bf16[128,2048]{1,0:T(8,128)(2,1)S(1)}, u32[]{:S(2)}, u32[]{:S(2)}) %collective-permute-start.1) | collective-permute-done | bytes 524320 | tf_op jit(solution)/shard_map/while/body/eval_jaxpr/ppermute | solution.py:259
  365.7 7.8 %collective-permute-done.1 = bf16[128,2048]{1,0:T(8,128)(2,1)S(1)} collective-permute-done((bf16[128,2048]{1,0:T(8,128)(2,1)}, bf16[128,2048]{1,0:T(8,128)(2,1)S(1)}, u32[]{:S(2)}, u32[]{:S(2)}) %collective-permute-start.1) | collective-permute-done | bytes 524320 | tf_op jit(solution)/shard_map/while/body/eval_jaxpr/ppermute | solution.py:259
  377.2 5.0 conditional.19
  377.4 4.7 fusion.69
  382.1 67.4 %collective-permute-done.1 = bf16[128,2048]{1,0:T(8,128)(2,1)S(1)} collective-permute-done((bf16[128,2048]{1,0:T(8,128)(2,1)}, bf16[128,2048]{1,0:T(8,128)(2,1)S(1)}, u32[]{:S(2)}, u32[]{:S(2)}) %collective-permute-start.1) | collective-permute-done | bytes 524320 | tf_op jit(solution)/shard_map/while/body/eval_jaxpr/ppermute | solution.py:259
  450.4 15.3 %conditional.18 = (bf16[128,2048]{1,0:T(8,128)(2,1)}, f32[2048]{0:T(1024)S(1)}) conditional(s32[]{:T(128)} %convert_element_type.349, () %tuple.188, (bf16[128,2048]{1,0:T(8,128)(2,1)S(1)}, bf16[1024,2048]{1,0:T(8,128)(2,1)}, s32[128]{0:T(128)S(1)}, f32[128,1536]{1,0:T(8,128)}, f32[128,1,32]{0,2,1:T(8,128)S(1)}, ...), branch_computations={%region_19.19_spmd, %region_20.28_spmd} | conditional | flops 1528560128 | bytes 55866488 | solution.py:256
  468.7 6.0 %collective-permute-done.1 = bf16[128,2048]{1,0:T(8,128)(2,1)S(1)} collective-permute-done((bf16[128,2048]{1,0:T(8,128)(2,1)}, bf16[128,2048]{1,0:T(8,128)(2,1)S(1)}, u32[]{:S(2)}, u32[]{:S(2)}) %collective-permute-start.1) | collective-permute-done | bytes 524320 | tf_op jit(solution)/shard_map/while/body/eval_jaxpr/ppermute | solution.py:259
  476.3 18.2 %collective-permute-start.1 = (bf16[128,2048]{1,0:T(8,128)(2,1)}, bf16[128,2048]{1,0:T(8,128)(2,1)S(1)}, u32[]{:S(2)}, u32[]{:S(2)}) collective-permute-start(bf16[128,2048]{1,0:T(8,128)(2,1)} %get-tuple-element.1275), channel_id=1, source_target_pairs={{32,0},{64,32},{96,64},{128,96},{160,128},{192,160},{224,192},{33,... | collective-permute-start | bytes 1572872 | tf_op jit(solution)/shard_map/while/body/eval_jaxpr/ppermute | solution.py:259
  495.5 6.0 %collective-permute-done.1 = bf16[128,2048]{1,0:T(8,128)(2,1)S(1)} collective-permute-done((bf16[128,2048]{1,0:T(8,128)(2,1)}, bf16[128,2048]{1,0:T(8,128)(2,1)S(1)}, u32[]{:S(2)}, u32[]{:S(2)}) %collective-permute-start.1) | collective-permute-done | bytes 524320 | tf_op jit(solution)/shard_map/while/body/eval_jaxpr/ppermute | solution.py:259
  503.2 3.8 collective-permute-start.1
  508.0 6.0 %collective-permute-done.1 = bf16[128,2048]{1,0:T(8,128)(2,1)S(1)} collective-permute-done((bf16[128,2048]{1,0:T(8,128)(2,1)}, bf16[128,2048]{1,0:T(8,128)(2,1)S(1)}, u32[]{:S(2)}, u32[]{:S(2)}) %collective-permute-start.1) | collective-permute-done | bytes 524320 | tf_op jit(solution)/shard_map/while/body/eval_jaxpr/ppermute | solution.py:259
  514.0 5.0 collective-permute-start.2
  527.2 5.8 %collective-permute-start.7 = (f32[2048]{0:T(1024)S(1)}, f32[2048]{0:T(1024)S(1)}, u32[]{:S(2)}, u32[]{:S(2)}) collective-permute-start(f32[2048]{0:T(1024)S(1)} %bitcast.250), channel_id=1, source_target_pairs={{0,12},{1,13},{2,14},{3,15},{4,8},{5,9},{6,10},{7,11},{8,4},{9,5},... | collective-permute-start | bytes 24584 | tf_op jit(solution)/shard_map/ppermute | solution.py:128
  (329 shorter events, 142.6 us)
Async XLA Ops:
  7.2 58.8 %copy-start.11 = (bf16[1,1024,64]{1,2,0:T(8,128)(2,1)S(1)}, bf16[1,1024,64]{1,2,0:T(8,128)(2,1)}, u32[]{:S(2)}) copy-start(bf16[1,1024,64]{1,2,0:T(8,128)(2,1)} %param.29) | copy-start | bytes 393220
  7.2 195.6 %all-gather.2.cloned.1.call-start = ((), (), s32[]{:S(2)}) async-start(), calls=%async_computation.2 | async-start | bytes 6488064 | tf_op jit(solution)/shard_map/all_gather | solution.py:179
  68.6 127.7 %all-to-all-start.1 = ((bf16[32,1024,64]{1,2,0:T(8,128)(2,1)}), bf16[32,1024,64]{1,2,0:T(8,128)(2,1)}, u32[]{:S(2)}, u32[]{:S(2)}) async-start(bf16[32,1024,64]{1,2,0:T(8,128)(2,1)} %stack.62), calls=%async_computation.1 | async-start | bytes 8388608 | tf_op jit(solution)/shard_map/all_to_all | solution.py:183
  79.4 123.4 %copy-start.1 = (f32[1,2048]{1,0:T(1,128)S(1)}, f32[1,2048]{1,0:T(1,128)}, u32[]{:S(2)}) copy-start(f32[1,2048]{1,0:T(1,128)} %param.26) | copy-start | bytes 24580
  79.4 123.4 %copy-start.5 = (f32[1,2048]{1,0:T(1,128)S(1)}, f32[1,2048]{1,0:T(1,128)}, u32[]{:S(2)}) copy-start(f32[1,2048]{1,0:T(1,128)} %param.25) | copy-start | bytes 24580
  204.3 10.5 %collective-permute-start = (bf16[128,2048]{1,0:T(8,128)(2,1)S(1)}, bf16[128,2048]{1,0:T(8,128)(2,1)S(1)}, u32[]{:S(2)}, u32[]{:S(2)}) collective-permute-start(bf16[128,2048]{1,0:T(8,128)(2,1)S(1)} %get-tuple-element.1378), channel_id=1, source_target_pairs={{0,32},{32,64},{64,96},{96,128},{128,160},{160,192},{192,224},{1,3... | collective-permute-start | bytes 1572872 | tf_op jit(solution)/shard_map/while/body/eval_jaxpr/ppermute | solution.py:237
  216.3 19.8 %collective-permute-start = (bf16[128,2048]{1,0:T(8,128)(2,1)S(1)}, bf16[128,2048]{1,0:T(8,128)(2,1)S(1)}, u32[]{:S(2)}, u32[]{:S(2)}) collective-permute-start(bf16[128,2048]{1,0:T(8,128)(2,1)S(1)} %get-tuple-element.1378), channel_id=1, source_target_pairs={{0,32},{32,64},{64,96},{96,128},{128,160},{160,192},{192,224},{1,3... | collective-permute-start | bytes 1572872 | tf_op jit(solution)/shard_map/while/body/eval_jaxpr/ppermute | solution.py:237
  246.6 10.5 %collective-permute-start = (bf16[128,2048]{1,0:T(8,128)(2,1)S(1)}, bf16[128,2048]{1,0:T(8,128)(2,1)S(1)}, u32[]{:S(2)}, u32[]{:S(2)}) collective-permute-start(bf16[128,2048]{1,0:T(8,128)(2,1)S(1)} %get-tuple-element.1378), channel_id=1, source_target_pairs={{0,32},{32,64},{64,96},{96,128},{128,160},{160,192},{192,224},{1,3... | collective-permute-start | bytes 1572872 | tf_op jit(solution)/shard_map/while/body/eval_jaxpr/ppermute | solution.py:237
  258.6 10.5 %collective-permute-start = (bf16[128,2048]{1,0:T(8,128)(2,1)S(1)}, bf16[128,2048]{1,0:T(8,128)(2,1)S(1)}, u32[]{:S(2)}, u32[]{:S(2)}) collective-permute-start(bf16[128,2048]{1,0:T(8,128)(2,1)S(1)} %get-tuple-element.1378), channel_id=1, source_target_pairs={{0,32},{32,64},{64,96},{96,128},{128,160},{160,192},{192,224},{1,3... | collective-permute-start | bytes 1572872 | tf_op jit(solution)/shard_map/while/body/eval_jaxpr/ppermute | solution.py:237
  270.6 10.5 %collective-permute-start = (bf16[128,2048]{1,0:T(8,128)(2,1)S(1)}, bf16[128,2048]{1,0:T(8,128)(2,1)S(1)}, u32[]{:S(2)}, u32[]{:S(2)}) collective-permute-start(bf16[128,2048]{1,0:T(8,128)(2,1)S(1)} %get-tuple-element.1378), channel_id=1, source_target_pairs={{0,32},{32,64},{64,96},{96,128},{128,160},{160,192},{192,224},{1,3... | collective-permute-start | bytes 1572872 | tf_op jit(solution)/shard_map/while/body/eval_jaxpr/ppermute | solution.py:237
  282.7 13.1 %collective-permute-start = (bf16[128,2048]{1,0:T(8,128)(2,1)S(1)}, bf16[128,2048]{1,0:T(8,128)(2,1)S(1)}, u32[]{:S(2)}, u32[]{:S(2)}) collective-permute-start(bf16[128,2048]{1,0:T(8,128)(2,1)S(1)} %get-tuple-element.1378), channel_id=1, source_target_pairs={{0,32},{32,64},{64,96},{96,128},{128,160},{160,192},{192,224},{1,3... | collective-permute-start | bytes 1572872 | tf_op jit(solution)/shard_map/while/body/eval_jaxpr/ppermute | solution.py:237
  297.3 10.5 %collective-permute-start = (bf16[128,2048]{1,0:T(8,128)(2,1)S(1)}, bf16[128,2048]{1,0:T(8,128)(2,1)S(1)}, u32[]{:S(2)}, u32[]{:S(2)}) collective-permute-start(bf16[128,2048]{1,0:T(8,128)(2,1)S(1)} %get-tuple-element.1378), channel_id=1, source_target_pairs={{0,32},{32,64},{64,96},{96,128},{128,160},{160,192},{192,224},{1,3... | collective-permute-start | bytes 1572872 | tf_op jit(solution)/shard_map/while/body/eval_jaxpr/ppermute | solution.py:237
  309.3 10.5 %collective-permute-start = (bf16[128,2048]{1,0:T(8,128)(2,1)S(1)}, bf16[128,2048]{1,0:T(8,128)(2,1)S(1)}, u32[]{:S(2)}, u32[]{:S(2)}) collective-permute-start(bf16[128,2048]{1,0:T(8,128)(2,1)S(1)} %get-tuple-element.1378), channel_id=1, source_target_pairs={{0,32},{32,64},{64,96},{96,128},{128,160},{160,192},{192,224},{1,3... | collective-permute-start | bytes 1572872 | tf_op jit(solution)/shard_map/while/body/eval_jaxpr/ppermute | solution.py:237
  322.6 10.0 %collective-permute-start.1 = (bf16[128,2048]{1,0:T(8,128)(2,1)}, bf16[128,2048]{1,0:T(8,128)(2,1)S(1)}, u32[]{:S(2)}, u32[]{:S(2)}) collective-permute-start(bf16[128,2048]{1,0:T(8,128)(2,1)} %get-tuple-element.1275), channel_id=1, source_target_pairs={{32,0},{64,32},{96,64},{128,96},{160,128},{192,160},{224,192},{33,... | collective-permute-start | bytes 1572872 | tf_op jit(solution)/shard_map/while/body/eval_jaxpr/ppermute | solution.py:259
  334.3 14.2 %collective-permute-start.1 = (bf16[128,2048]{1,0:T(8,128)(2,1)}, bf16[128,2048]{1,0:T(8,128)(2,1)S(1)}, u32[]{:S(2)}, u32[]{:S(2)}) collective-permute-start(bf16[128,2048]{1,0:T(8,128)(2,1)} %get-tuple-element.1275), channel_id=1, source_target_pairs={{32,0},{64,32},{96,64},{128,96},{160,128},{192,160},{224,192},{33,... | collective-permute-start | bytes 1572872 | tf_op jit(solution)/shard_map/while/body/eval_jaxpr/ppermute | solution.py:259
  350.1 10.8 %collective-permute-start.1 = (bf16[128,2048]{1,0:T(8,128)(2,1)}, bf16[128,2048]{1,0:T(8,128)(2,1)S(1)}, u32[]{:S(2)}, u32[]{:S(2)}) collective-permute-start(bf16[128,2048]{1,0:T(8,128)(2,1)} %get-tuple-element.1275), channel_id=1, source_target_pairs={{32,0},{64,32},{96,64},{128,96},{160,128},{192,160},{224,192},{33,... | collective-permute-start | bytes 1572872 | tf_op jit(solution)/shard_map/while/body/eval_jaxpr/ppermute | solution.py:259
  362.6 10.8 %collective-permute-start.1 = (bf16[128,2048]{1,0:T(8,128)(2,1)}, bf16[128,2048]{1,0:T(8,128)(2,1)S(1)}, u32[]{:S(2)}, u32[]{:S(2)}) collective-permute-start(bf16[128,2048]{1,0:T(8,128)(2,1)} %get-tuple-element.1275), channel_id=1, source_target_pairs={{32,0},{64,32},{96,64},{128,96},{160,128},{192,160},{224,192},{33,... | collective-permute-start | bytes 1572872 | tf_op jit(solution)/shard_map/while/body/eval_jaxpr/ppermute | solution.py:259
  375.1 74.5 %copy-start.10 = (s32[128]{0:T(128)S(1)}, s32[128]{0:T(128)}, u32[]{:S(2)}) copy-start(s32[128]{0:T(128)} %get-tuple-element.1415) | copy-start | bytes 1540 | tf_op jit(solution)/shard_map/while
  375.1 74.5 %collective-permute-start.1 = (bf16[128,2048]{1,0:T(8,128)(2,1)}, bf16[128,2048]{1,0:T(8,128)(2,1)S(1)}, u32[]{:S(2)}, u32[]{:S(2)}) collective-permute-start(bf16[128,2048]{1,0:T(8,128)(2,1)} %get-tuple-element.1275), channel_id=1, source_target_pairs={{32,0},{64,32},{96,64},{128,96},{160,128},{192,160},{224,192},{33,... | collective-permute-start | bytes 1572872 | tf_op jit(solution)/shard_map/while/body/eval_jaxpr/ppermute | solution.py:259
  382.1 67.5 %copy-start.7 = (f32[2048]{0:T(1024)}, f32[2048]{0:T(1024)S(1)}, u32[]{:S(2)}) copy-start(f32[2048]{0:T(1024)S(1)} %select_add_fusion.2) | copy-start | bytes 24580 | tf_op jit(solution)/shard_map/while
  465.6 9.0 %collective-permute-start.1 = (bf16[128,2048]{1,0:T(8,128)(2,1)}, bf16[128,2048]{1,0:T(8,128)(2,1)S(1)}, u32[]{:S(2)}, u32[]{:S(2)}) collective-permute-start(bf16[128,2048]{1,0:T(8,128)(2,1)} %get-tuple-element.1275), channel_id=1, source_target_pairs={{32,0},{64,32},{96,64},{128,96},{160,128},{192,160},{224,192},{33,... | collective-permute-start | bytes 1572872 | tf_op jit(solution)/shard_map/while/body/eval_jaxpr/ppermute | solution.py:259
  476.3 19.2 %copy-start.6 = (f32[2048]{0:T(1024)S(1)}, f32[2048]{0:T(1024)}, u32[]{:S(2)}) copy-start(f32[2048]{0:T(1024)} %get-tuple-element.1343) | copy-start | bytes 24580 | tf_op jit(solution)/shard_map/while
  476.3 25.2 %copy-start.10 = (s32[128]{0:T(128)S(1)}, s32[128]{0:T(128)}, u32[]{:S(2)}) copy-start(s32[128]{0:T(128)} %get-tuple-element.1415) | copy-start | bytes 1540 | tf_op jit(solution)/shard_map/while
  476.3 25.2 %collective-permute-start.1 = (bf16[128,2048]{1,0:T(8,128)(2,1)}, bf16[128,2048]{1,0:T(8,128)(2,1)S(1)}, u32[]{:S(2)}, u32[]{:S(2)}) collective-permute-start(bf16[128,2048]{1,0:T(8,128)(2,1)} %get-tuple-element.1275), channel_id=1, source_target_pairs={{32,0},{64,32},{96,64},{128,96},{160,128},{192,160},{224,192},{33,... | collective-permute-start | bytes 1572872 | tf_op jit(solution)/shard_map/while/body/eval_jaxpr/ppermute | solution.py:259
  503.2 10.8 %collective-permute-start.1 = (bf16[128,2048]{1,0:T(8,128)(2,1)}, bf16[128,2048]{1,0:T(8,128)(2,1)S(1)}, u32[]{:S(2)}, u32[]{:S(2)}) collective-permute-start(bf16[128,2048]{1,0:T(8,128)(2,1)} %get-tuple-element.1275), channel_id=1, source_target_pairs={{32,0},{64,32},{96,64},{128,96},{160,128},{192,160},{224,192},{33,... | collective-permute-start | bytes 1572872 | tf_op jit(solution)/shard_map/while/body/eval_jaxpr/ppermute | solution.py:259
  514.0 7.4 %collective-permute-start.2 = (f32[2048]{0:T(1024)}, f32[2048]{0:T(1024)S(1)}, u32[]{:S(2)}, u32[]{:S(2)}) collective-permute-start(f32[2048]{0:T(1024)} %get-tuple-element.1399), channel_id=1, source_target_pairs={{0,1},{1,0},{2,3},{3,2},{4,5},{5,4},{6,7},{7,6},{8,9},{9,8},{10,11... | collective-permute-start | bytes 24584 | tf_op jit(solution)/shard_map/ppermute | solution.py:128
  519.0 4.8 collective-permute-start.3
  519.0 5.7 %collective-permute-start.4 = (f32[2048]{0:T(1024)}, f32[2048]{0:T(1024)S(1)}, u32[]{:S(2)}, u32[]{:S(2)}) collective-permute-start(f32[2048]{0:T(1024)} %get-tuple-element.1399), channel_id=1, source_target_pairs={{0,3},{1,2},{2,1},{3,0},{4,7},{5,6},{6,5},{7,4},{8,11},{9,10},{10,... | collective-permute-start | bytes 24584 | tf_op jit(solution)/shard_map/ppermute | solution.py:128
  525.5 7.6 %collective-permute-start.5 = (f32[2048]{0:T(1024)S(1)}, f32[2048]{0:T(1024)S(1)}, u32[]{:S(2)}, u32[]{:S(2)}) collective-permute-start(f32[2048]{0:T(1024)S(1)} %bitcast.248), channel_id=1, source_target_pairs={{0,4},{1,5},{2,6},{3,7},{4,0},{5,1},{6,2},{7,3},{8,12},{9,13},{10,... | collective-permute-start | bytes 24584 | tf_op jit(solution)/shard_map/ppermute | solution.py:128
  526.9 6.2 %collective-permute-start.6 = (f32[2048]{0:T(1024)S(1)}, f32[2048]{0:T(1024)S(1)}, u32[]{:S(2)}, u32[]{:S(2)}) collective-permute-start(f32[2048]{0:T(1024)S(1)} %bitcast.249), channel_id=1, source_target_pairs={{0,8},{1,9},{2,10},{3,11},{4,12},{5,13},{6,14},{7,15},{8,0},{9,1},... | collective-permute-start | bytes 24584 | tf_op jit(solution)/shard_map/ppermute | solution.py:128
  527.2 8.5 %collective-permute-start.7 = (f32[2048]{0:T(1024)S(1)}, f32[2048]{0:T(1024)S(1)}, u32[]{:S(2)}, u32[]{:S(2)}) collective-permute-start(f32[2048]{0:T(1024)S(1)} %bitcast.250), channel_id=1, source_target_pairs={{0,12},{1,13},{2,14},{3,15},{4,8},{5,9},{6,10},{7,11},{8,4},{9,5},... | collective-permute-start | bytes 24584 | tf_op jit(solution)/shard_map/ppermute | solution.py:128
  535.7 5.2 collective-permute-start.8
  (29 other events, 175.6 us)
Sparse Core Ops, SparseCore 0:
  10.6 163.5 all-gather.1
